TPU v7x, 512 devices: a whole 4x8x8 slice. The times are simulated.
512 devices in a mesh: req: 128 (over z, y, core), grp: 4 (over x).
Axes of the slice: x: 4, y: 8, z: 8, core: 2. Of those that a mesh axis runs over, the one named last changes fastest.
Arguments:
- owner_slab: bfloat16 [65536, 1024], P('req'), may hold values from -6 to 6
- segment_ids: int32 [128, 512], P('req'), may hold values from 0 to 511, as said below
- head_weights: bfloat16 [1024, 16, 192], P(None, 'grp')
- merge_weights: bfloat16 [16, 64, 1024], P('grp'), may hold values from -0.1875 to 0.1875
- first_gain: float32 [1024], replicated, may hold values from 0.25 to 1.75
- first_bias: float32 [1024], replicated, may hold values from -3 to 3
- up_weights: bfloat16 [1024, 4096], P('req', 'grp'), may hold values from -0.1875 to 0.1875
- down_weights: bfloat16 [4096, 1024], P('grp', 'req'), may hold values from -0.09375 to 0.09375
- second_gain: float32 [1024], replicated, may hold values from 0.25 to 1.75
- second_bias: float32 [1024], replicated, may hold values from -3 to 3
- page_table: int32 [128, 4], P('req'), may hold values from 0 to 3, each once within a row
- row_map: int32 [128, 4, 128], P('req', 'grp'), may hold values from 0 to 127, each once within a row
Outputs:
- layer_out: bfloat16 [65536, 1024], P(('req', 'grp'))
- cache_pages: bfloat16 [512, 128, 16, 128], P('req', None, 'grp')
Inputs may be any that keep to these rules, and one draw needn't show every extreme that they name: `segment_ids`: within each slab the ids start at 0, never fall and rise by at most one from row to row; in one slab all 512 rows form a single request, and in one other slab every row is a request of its own.
All inputs are finite; a program needn't handle non-finite values.
Results may differ from a plain program's by a relative error of at most 0.0075.
Values may be sent and summed in bfloat16 or wider, within the bound.
No kernel may reach another device: no remote copies, remote signals or barrier semaphores. Data moves between devices by JAX's collectives and lax.ppermute only.
A program may use at most 64 MiB of HBM per device.

v0:
```python
import math
import jax
import jax.numpy as jnp
import numpy as np
from jax import lax
from jax.sharding import Mesh
from jax.sharding import PartitionSpec as P

EPSILON = 1e-05
REQ = ("rz", "ry", "rc")


def layer_norm(values, gain, bias):
    center = values - jnp.mean(values, axis=-1, keepdims=True)
    spread = jnp.mean(center * center, axis=-1, keepdims=True)
    return center * lax.rsqrt(spread + EPSILON) * gain + bias


def split_req(mesh):
    column = mesh.devices[:, 0]
    try:
        cores = len({d.core_on_chip for d in column})
        ys = len({d.coords[1] for d in column})
        zs = len({d.coords[2] for d in column})
    except AttributeError:
        return (column.shape[0], 1, 1)
    if zs * ys * cores != column.shape[0]:
        return (column.shape[0], 1, 1)
    return (zs, ys, cores)


def gather_rows(block, first, second):
    a = lax.all_gather(block, first, axis=0, tiled=False)
    b = lax.all_gather(a, second, axis=0, tiled=False)
    c = lax.all_gather(b, "rc", axis=0, tiled=False)
    if first == "ry":
        c = jnp.transpose(c, (1, 2, 0, 3, 4))
    else:
        c = jnp.transpose(c, (2, 1, 0, 3, 4))
    return c.reshape(-1, block.shape[1])


def local(
    owner_slab,
    segment_ids,
    head_weights,
    merge_weights,
    first_gain,
    first_bias,
    up_weights,
    down_weights,
    second_gain,
    second_bias,
    page_table,
    row_map,
):
    group = lax.axis_size("grp")
    owners = lax.axis_size(REQ)
    zs = lax.axis_size("rz")
    rows_all = owner_slab.shape[0]
    width = owner_slab.shape[1]
    quarter = rows_all // group
    local_heads = head_weights.shape[1]
    head_dim = head_weights.shape[2] // 3
    up_full = gather_rows(up_weights, "ry", "rz")
    down_full_t = gather_rows(jnp.transpose(down_weights), "rz", "ry")
    projected = jnp.einsum(
        "nd,dhc->nhc", owner_slab, head_weights, preferred_element_type=jnp.float32
    ).astype(jnp.bfloat16)
    queries = jnp.moveaxis(projected[:, :, :head_dim], 1, 0)
    key_rows = jnp.moveaxis(projected[:, :, head_dim : 2 * head_dim], 1, 0)
    value_rows = jnp.moveaxis(projected[:, :, 2 * head_dim :], 1, 0)
    segment = segment_ids[0]
    position = jnp.arange(rows_all, dtype=jnp.int32)
    allowed = (position[:, None] >= position[None, :]) & (segment[:, None] == segment[None, :])
    scale = 1.0 / math.sqrt(head_dim)

    def one_head(operands):
        query_head, key_head, value_head = operands
        scores = (
            lax.dot_general(
                query_head, key_head, (((1,), (1,)), ((), ())), preferred_element_type=jnp.float32
            )
            * scale
        )
        scores = jnp.where(allowed, scores, -1e30)
        probs = jax.nn.softmax(scores, axis=-1).astype(jnp.bfloat16)
        return jnp.dot(probs, value_head, preferred_element_type=jnp.float32).astype(jnp.bfloat16)

    attended = jnp.moveaxis(lax.map(one_head, (queries, key_rows, value_rows)), 0, 1)
    own = lax.axis_index("grp")
    own_rows = lax.dynamic_slice_in_dim(owner_slab, own * quarter, quarter, 0).astype(jnp.float32)
    partial_rows = jnp.einsum(
        "nhd,hde->ne", attended, merge_weights, preferred_element_type=jnp.float32
    )
    mixed = lax.psum_scatter(partial_rows, "grp", scatter_dimension=0, tiled=True)
    hidden = layer_norm(own_rows + mixed, first_gain, first_bias).astype(jnp.bfloat16)
    slots = quarter // owners
    placed = jnp.zeros_like(hidden).at[row_map[0, 0]].set(hidden)
    staged = placed.reshape(zs, owners // zs, slots * width)
    staged = lax.all_to_all(staged, "rz", split_axis=0, concat_axis=0, tiled=True)
    staged = lax.all_to_all(staged, ("ry", "rc"), split_axis=1, concat_axis=1, tiled=True)
    even_rows = staged.reshape(quarter, width)
    group_rows = lax.all_gather(even_rows, "grp", axis=0, tiled=True)
    raised = jnp.dot(group_rows, up_full, preferred_element_type=jnp.float32)
    activated = jax.nn.gelu(raised, approximate=False).astype(jnp.bfloat16)
    lowered_all = lax.dot_general(
        activated, down_full_t, (((1,), (1,)), ((), ())), preferred_element_type=jnp.float32
    )
    lowered = lax.psum_scatter(lowered_all, "grp", scatter_dimension=0, tiled=True)
    layer_out = layer_norm(
        even_rows.astype(jnp.float32) + lowered, second_gain, second_bias
    ).astype(jnp.bfloat16)
    page_count = page_table.shape[1]
    page_rows = rows_all // page_count
    stacked = projected[:, :, head_dim:].reshape(page_count, page_rows, local_heads, 2 * head_dim)
    cache_pages = jnp.zeros_like(stacked).at[page_table[0]].set(stacked)
    return (layer_out, cache_pages)


def solution(mesh):
    zs, ys, cores = split_req(mesh)
    devices = np.asarray(mesh.devices).reshape(zs, ys, cores, mesh.devices.shape[1])
    inner = Mesh(devices, REQ + ("grp",))
    in_specs = (
        P(REQ, None),
        P(REQ, None),
        P(None, "grp", None),
        P("grp", None, None),
        P(),
        P(),
        P(REQ, "grp"),
        P("grp", REQ),
        P(),
        P(),
        P(REQ, None),
        P(REQ, "grp", None),
    )
    out_specs = (P(REQ + ("grp",), None), P(REQ, None, "grp", None))
    return jax.shard_map(local, mesh=inner, in_specs=in_specs, out_specs=out_specs, check_vma=False)
```

profile of v0, /device:TPU:1, one launch (start us, length us, event | category | flops | bytes accessed | tf_op | source)
XLA Modules:
  0.0 255.3 jit_solution(2603240170650563449)
XLA Ops:
  8.1 23.0 %all-gather = bf16[64,1024]{1,0:T(8,128)(2,1)} all-gather(bf16[8,1024]{1,0:T(8,128)(2,1)} %param.20), channel_id=2, replica_groups=mesh['rz'=8,'ry'=8,'rc'=2,'grp'=4] {'ry'}, dimensions={0}, use_global_device_ids=true | all-gather | bytes 147456 | tf_op jit(solution)/shard_map/all_gather | solution.py:33
  31.1 27.1 %all-gather.3 = bf16[64,1024]{1,0:T(8,128)(2,1)} all-gather(bf16[8,1024]{1,0:T(8,128)(2,1)} %bitcast.90), channel_id=5, replica_groups=mesh['rz'=8,'ry'=8,'rc'=2,'grp'=4] {'rz'}, dimensions={0}, use_global_device_ids=true | all-gather | bytes 147456 | tf_op jit(solution)/shard_map/all_gather | solution.py:33
  58.3 2.2 fusion.101
  60.7 0.5 copy-done.7
  61.2 3.7 %while.11 = (s32[]{:T(128)}, bf16[4,512,64]{1,2,0:T(8,128)(2,1)S(1)}, bf16[4,512,64]{1,2,0:T(8,128)(2,1)S(1)}, bf16[4,512,64]{1,2,0:T(8,128)(2,1)S(1)}, bf16[4,5...) while((s32[]{:T(128)}, bf16[4,512,64]{1,2,0:T(8,128)(2,1)S(1)}, ...), condition=%wide.region_3.4_spmd.clone, body=%wide.region_0.3_spmd.clone.sunk | while | flops 70024192 | bytes 3424341 | solution.py:90
  61.2 0.4 fusion.113
  62.1 0.4 fusion.113
  62.7 0.3 fusion.115
  63.1 0.4 fusion.113
  63.7 0.3 fusion.115
  64.0 0.4 fusion.113
  64.6 0.3 fusion.115
  64.9 2.8 %convolution_bitcast_fusion = f32[512,1024]{1,0:T(8,128)} fusion(bf16[4,64,1024]{2,1,0:T(8,128)(2,1)} %param.17, bf16[4,512,64]{1,2,0:T(8,128)(2,1)S(1)} %get-tuple-element.34), kind=kOutput, calls=%fused_computation.40 | convolution fusion | flops 268435456 | bytes 2883584 | tf_op jit(solution)/shard_map/nhd,hde->ne/dot_general | solution.py:93
  67.9 10.0 %all-gather.14.cloned.1.call-done = bf16[64,8,1024]{2,1,0:T(8,128)(2,1)} async-done(((bf16[8,8,1024]{2,1,0:T(8,128)(2,1)}), bf16[64,8,1024]{2,1,0:T(8,128)(2,1)}) %all-gather.14.cloned.1.call-update) | async-done | bytes 1048592 | tf_op jit(solution)/shard_map/all_gather | solution.py:34
  78.0 41.6 %all-gather.18.cloned.1.call-done = bf16[64,8,1024]{2,1,0:T(8,128)(2,1)} async-done(((bf16[8,8,1024]{2,1,0:T(8,128)(2,1)}), bf16[64,8,1024]{2,1,0:T(8,128)(2,1)}) %all-gather.18.cloned.1.call-update) | async-done | bytes 1048592 | tf_op jit(solution)/shard_map/all_gather | solution.py:34
  119.7 1.2 fusion.64
  120.9 1.2 multiply_reduce_fusion.1
  122.2 1.9 scatter_custom_fusion
  124.1 16.0 %all_to_all.10 = bf16[8,16,1024]{2,1,0:T(8,128)(2,1)S(1)} all-to-all(bf16[8,16,1024]{2,1,0:T(8,128)(2,1)S(1)} %bitcast.87), channel_id=1, replica_groups=mesh['rz'=8,'ry'=8,'rc'=2,'grp'=4] {'rz'}, dimensions={0} | all-to-all | bytes 524288 | tf_op jit(solution)/shard_map/all_to_all | solution.py:101
  140.3 21.8 %all_to_all.11 = bf16[8,16,1024]{2,0,1:T(8,128)(2,1)S(1)} all-to-all(bf16[8,16,1024]{2,0,1:T(8,128)(2,1)S(1)} %copy.42), channel_id=1, replica_groups=mesh['rz'=8,'ry'=8,'rc'=2,'grp'=4] {'ry','rc'}, dimensions={1} | all-to-all | bytes 524288 | tf_op jit(solution)/shard_map/all_to_all | solution.py:102
  162.1 0.9 copy.43
  163.2 3.2 %copy.44 = bf16[8,8,2,8,1024]{4,3,2,1,0:T(8,128)(2,1)} copy(bf16[8,8,2,8,1024]{4,3,1,0,2:T(8,128)(2,1)} %bitcast.80) | data formatting | bytes 4194304 | tf_op jit(solution)/shard_map/transpose | solution.py:37
  166.5 3.1 %copy.45 = bf16[8,8,2,8,1024]{4,3,2,1,0:T(8,128)(2,1)} copy(bf16[8,8,2,8,1024]{4,3,0,1,2:T(8,128)(2,1)} %bitcast.81) | data formatting | bytes 4194304 | tf_op jit(solution)/shard_map/transpose | solution.py:39
  169.6 26.6 %all-gather.12.cloned.1.call-done = bf16[512,1024]{1,0:T(8,128)(2,1)} async-done(((bf16[128,1024]{1,0:T(8,128)(2,1)}), bf16[512,1024]{1,0:T(8,128)(2,1)}) %all-gather.12.cloned.1.call-update) | async-done | bytes 1048592 | tf_op jit(solution)/shard_map/all_gather | solution.py:104
  196.3 10.1 %fusion.25 = f32[512,1024]{1,0:T(8,128)} fusion(bf16[1024,1024]{1,0:T(8,128)(2,1)} %bitcast.83, bf16[512,1024]{1,0:T(8,128)(2,1)} %all-gather.12.cloned.1.call-done, bf16[1024,1024]{1,0:T(8,128)(2,1)} %bitcast.82), kind=kOutput, calls=%fused_computation.41 | convolution fusion | flops 2181562368 | bytes 7340032 | tf_op jit(solution)/shard_map/dot_general | solution.py:107
  206.6 0.4 copy.46
  207.2 0.8 scatter_fusion
  208.0 1.2 copy.47
  209.2 34.7 %reduce-scatter.5.cloned.1.call-done = f32[128,1024]{1,0:T(8,128)} async-done(((f32[512,1024]{1,0:T(8,128)}), f32[128,1024]{1,0:T(8,128)}) %reduce-scatter.5.cloned.1.call-update) | async-done | bytes 524304 | tf_op jit(solution)/shard_map/reduce_scatter | solution.py:110
  243.9 1.2 fusion.63
  245.0 1.2 multiply_reduce_fusion
  246.3 1.9 add_convert_fusion
  (54 shorter events, 2.6 us)
Async XLA Ops:
  8.0 50.3 %copy-start = (bf16[1024,4,192]{0,2,1:T(8,128)(2,1)S(1)}, bf16[1024,4,192]{0,2,1:T(8,128)(2,1)}, u32[]{:S(2)}) copy-start(bf16[1024,4,192]{0,2,1:T(8,128)(2,1)} %param.16) | copy-start | bytes 4718596
  8.0 69.9 %all-gather.14.cloned.1.call-start = ((), (), s32[]{:S(2)}) async-start(), calls=%async_computation.7 | async-start | bytes 1179648 | tf_op jit(solution)/shard_map/all_gather | solution.py:34
  31.1 88.5 %all-gather.18.cloned.1.call-start = ((), (), s32[]{:S(2)}) async-start(), calls=%async_computation.9 | async-start | bytes 1179648 | tf_op jit(solution)/shard_map/all_gather | solution.py:34
  58.2 61.5 %reduce-scatter.3.cloned.1.call-start = ((), (), s32[]{:S(2)}) async-start(), calls=%async_computation.4 | async-start | bytes 2621440 | tf_op jit(solution)/shard_map/reduce_scatter | solution.py:96
  60.5 0.7 copy-start.7
  67.8 51.9 %copy-start.8 = (s32[1,1,128]{2,1,0:T(1,128)S(1)}, s32[1,1,128]{2,1,0:T(1,128)}, u32[]{:S(2)}) copy-start(s32[1,1,128]{2,1,0:T(1,128)} %param.25) | copy-start | bytes 1540
  67.8 51.9 %copy-start.2 = (bf16[512,1024]{1,0:T(8,128)(2,1)S(1)}, bf16[512,1024]{1,0:T(8,128)(2,1)}, u32[]{:S(2)}) copy-start(bf16[512,1024]{1,0:T(8,128)(2,1)} %param.14) | copy-start | bytes 3145732
  67.8 54.4 %copy-start.3 = (f32[1024]{0:T(1024)S(1)}, f32[1024]{0:T(1024)}, u32[]{:S(2)}) copy-start(f32[1024]{0:T(1024)} %param.19) | copy-start | bytes 12292
  67.8 54.4 %copy-start.4 = (f32[1024]{0:T(1024)S(1)}, f32[1024]{0:T(1024)}, u32[]{:S(2)}) copy-start(f32[1024]{0:T(1024)} %param.18) | copy-start | bytes 12292
  67.8 95.4 %all-gather.16.cloned.1.call-start = ((), (), s32[]{:S(2)}) async-start(), calls=%async_computation.8 | async-start | bytes 3145728 | tf_op jit(solution)/shard_map/all_gather | solution.py:35
  78.0 88.5 %all-gather.20.cloned.1.call-start = ((), (), s32[]{:S(2)}) async-start(), calls=%async_computation.10 | async-start | bytes 3145728 | tf_op jit(solution)/shard_map/all_gather | solution.py:35
  119.6 76.6 %all-gather.12.cloned.1.call-start = ((), (), s32[]{:S(2)}) async-start(), calls=%async_computation.5 | async-start | bytes 1310720 | tf_op jit(solution)/shard_map/all_gather | solution.py:104
  162.9 80.9 %reduce-scatter.5.cloned.1.call-start = ((), (), s32[]{:S(2)}) async-start(), calls=%async_computation.6 | async-start | bytes 2621440 | tf_op jit(solution)/shard_map/reduce_scatter | solution.py:110
  206.4 0.7 copy-start.9
  206.6 37.3 %copy-start.1 = (bf16[8,16,1024]{2,1,0:T(8,128)(2,1)S(1)}, bf16[8,16,1024]{2,1,0:T(8,128)(2,1)}, u32[]{:S(2)}) copy-start(bf16[8,16,1024]{2,1,0:T(8,128)(2,1)} %copy.43) | copy-start | bytes 786436
  207.2 39.1 %copy-start.5 = (f32[1024]{0:T(1024)S(1)}, f32[1024]{0:T(1024)}, u32[]{:S(2)}) copy-start(f32[1024]{0:T(1024)} %param.23) | copy-start | bytes 12292
  207.2 39.1 %copy-start.6 = (f32[1024]{0:T(1024)S(1)}, f32[1024]{0:T(1024)}, u32[]{:S(2)}) copy-start(f32[1024]{0:T(1024)} %param.22) | copy-start | bytes 12292
Sparse Core Ops, SparseCore 0:
  31.2 46.7 all-gather.13
  80.0 39.5 all-gather.17
  121.7 22.7 all-gather.15
  146.4 20.0 all-gather.19
  169.0 27.1 all-gather.11
Sparse Core Ops, SparseCore 1:
  67.9 44.0 reduce-scatter.2
  206.5 37.3 reduce-scatter.4
where the time goes:
time: 256 us; the launch traced here: 255 us
  waiting for transfers between devices  113 us (44%)
  blocking collectives  87.8 us (34%)
  matrix products  18.1 us (7%)
  between operations  15.5 us (6%)
  local copies, waits for them, and re-layouts  10.6 us (4%)
  other arithmetic  9.59 us (4%)
    all_gather x2, waiting for transfers between devices, gather_rows(): b = lax.all_gather(a, second, axis=0, tiled=False)  51.6 us
    all_gather x2, blocking collectives, gather_rows(): a = lax.all_gather(block, first, axis=0, tiled=False)  50 us
    reduce_scatter x1, waiting for transfers between devices, local(): lax.psum_scatter(lowered_all, 'grp', scatter_dimension=0, tiled=True)  34.7 us
    all_gather x1, waiting for transfers between devices, local(): group_rows = lax.all_gather(even_rows, 'grp', axis=0, tiled=True)  26.6 us
    all_to_all x1, blocking collectives, local(): lax.all_to_all(staged, ('ry', 'rc'), split_axis=1, concat_axis=1, tiled=T...  21.8 us
    all_to_all x1, blocking collectives, local(): lax.all_to_all(staged, 'rz', split_axis=0, concat_axis=0, tiled=True)  16 us
    dot_general x1, matrix products, local(): lax.dot_general(activated, down_full_t, (((1,), (1,)), ((), ())), preferr...  10.1 us
  transfers between devices with their start and end apart: 7, of which 5 were waited for; matrix products, arithmetic and copies ran while one was open for 9% of the time, Pallas kernels for 0%

commit v1 on v0

--- a/solution.py
+++ b/solution.py
@@ -5,9 +5,17 @@
 from jax import lax
 from jax.sharding import Mesh
 from jax.sharding import PartitionSpec as P
+from jax.lax import axis_index, axis_size, ppermute
 
 EPSILON = 1e-05
 REQ = ("rz", "ry", "rc")
+
+
+def close_zone_now(here_x, dim_i):
+    here_x = jnp.moveaxis(here_x, 0, dim_i)
+    t1 = here_x.shape
+    z2 = here_x.reshape(*t1[:dim_i], t1[dim_i] * t1[dim_i + 1], *t1[dim_i + 2 :])
+    return z2
 
 
 def layer_norm(values, gain, bias):
@@ -101,7 +109,24 @@
     staged = lax.all_to_all(staged, "rz", split_axis=0, concat_axis=0, tiled=True)
     staged = lax.all_to_all(staged, ("ry", "rc"), split_axis=1, concat_axis=1, tiled=True)
     even_rows = staged.reshape(quarter, width)
-    group_rows = lax.all_gather(even_rows, "grp", axis=0, tiled=True)
+
+    def _move_boxes(load, bus_axis, axis_k):
+        nodes = axis_size(bus_axis)
+        windows = [(nth, (nth + 1) % nodes) for nth in range(nodes)]
+        moved, arr_now = ([], [])
+        table = [(tick, ii) for ii, tick in windows]
+        for dev_i in range(nodes - 1):
+            if dev_i % 2 == 0:
+                moved.append(ppermute(moved[-1] if moved else load, bus_axis, windows))
+            else:
+                arr_now.append(ppermute(arr_now[-1] if arr_now else load, bus_axis, table))
+        y2 = jnp.stack([*moved[::-1], load, *arr_now], 0)
+        part_now = axis_index(bus_axis) - len(moved)
+        y2 = y2[(jnp.arange(nodes) - part_now) % nodes]
+        x_next = close_zone_now(y2, axis_k)
+        return x_next
+
+    group_rows = _move_boxes(even_rows, "grp", axis_k=0)
     raised = jnp.dot(group_rows, up_full, preferred_element_type=jnp.float32)
     activated = jax.nn.gelu(raised, approximate=False).astype(jnp.bfloat16)
     lowered_all = lax.dot_general(

time: 256 us -> 235 us (0.918)
  waiting for transfers between devices: 113 us -> 80.5 us
  starting transfers between devices: 0.46 us -> 8.83 us
    all_gather x1 -> x0, waiting for transfers between devices: 26.6 us -> none  [local(): group_rows = lax.all_gather(even_rows, 'grp', axis=0, tiled=True)]
    reduce_scatter x1, waiting for transfers between devices: 34.7 us -> 22 us  [local(): lax.psum_scatter(lowered_all, 'grp', scatter_dimension=0, tiled=True)]
    ppermute x0 -> x3, starting transfers between devices: none -> 8.58 us  [the longest x2 5.14 us: _move_boxes(): moved.append(ppermute(moved[-1] if moved else load, bus_axis, windows))]
    ppermute x0 -> x3, waiting for transfers between devices: none -> 6.75 us  [the longest x2 6.74 us: _move_boxes(): moved.append(ppermute(moved[-1] if moved else load, bus_axis, windows))]
    gather x0 -> x1, local copies, waits for them, and re-layouts: none -> 2.83 us  [_move_boxes(): y2 = y2[(jnp.arange(nodes) - part_now) % nodes]]
  transfers between devices with their start and end apart: 7 -> 9, of which waited for: 5 -> 5; matrix products, arithmetic and copies ran while one was open for 9% -> 10% of each run, Pallas kernels for 0% -> 0%
where the time goes in v1:
time: 235 us; the launch traced here: 234 us
  blocking collectives  87.8 us (37%)
  waiting for transfers between devices  80.5 us (34%)
  matrix products  18.1 us (8%)
  between operations  15.5 us (7%)
  local copies, waits for them, and re-layouts  12.8 us (5%)
  other arithmetic  10.7 us (5%)
  starting transfers between devices  8.83 us (4%)
    all_gather x2, waiting for transfers between devices, gather_rows(): b = lax.all_gather(a, second, axis=0, tiled=False)  51.6 us
    all_gather x2, blocking collectives, gather_rows(): a = lax.all_gather(block, first, axis=0, tiled=False)  50 us
    reduce_scatter x1, waiting for transfers between devices, local(): lax.psum_scatter(lowered_all, 'grp', scatter_dimension=0, tiled=True)  22 us
    all_to_all x1, blocking collectives, local(): lax.all_to_all(staged, ('ry', 'rc'), split_axis=1, concat_axis=1, tiled=T...  21.8 us
    all_to_all x1, blocking collectives, local(): lax.all_to_all(staged, 'rz', split_axis=0, concat_axis=0, tiled=True)  16 us
    dot_general x1, matrix products, local(): lax.dot_general(activated, down_full_t, (((1,), (1,)), ((), ())), preferr...  10.1 us
    ppermute x2, waiting for transfers between devices, _move_boxes(): moved.append(ppermute(moved[-1] if moved else load, bus_axis, windows))  6.74 us
    ppermute x2, starting transfers between devices, _move_boxes(): moved.append(ppermute(moved[-1] if moved else load, bus_axis, windows))  5.14 us
  transfers between devices with their start and end apart: 9, of which 5 were waited for; matrix products, arithmetic and copies ran while one was open for 10% of the time, Pallas kernels for 0%

profile of v1, /device:TPU:1, one launch (start us, length us, event | category | flops | bytes accessed | tf_op | source)
XLA Modules:
  0.0 234.2 jit_solution(345942135970446218)
XLA Ops:
  8.1 23.0 %all-gather = bf16[64,1024]{1,0:T(8,128)(2,1)} all-gather(bf16[8,1024]{1,0:T(8,128)(2,1)} %param.20), channel_id=2, replica_groups=mesh['rz'=8,'ry'=8,'rc'=2,'grp'=4] {'ry'}, dimensions={0}, use_global_device_ids=true | all-gather | bytes 147456 | tf_op jit(solution)/shard_map/all_gather | solution.py:41
  31.1 27.1 %all-gather.3 = bf16[64,1024]{1,0:T(8,128)(2,1)} all-gather(bf16[8,1024]{1,0:T(8,128)(2,1)} %bitcast.103), channel_id=5, replica_groups=mesh['rz'=8,'ry'=8,'rc'=2,'grp'=4] {'rz'}, dimensions={0}, use_global_device_ids=true | all-gather | bytes 147456 | tf_op jit(solution)/shard_map/all_gather | solution.py:41
  58.3 2.2 fusion.103
  60.7 0.5 copy-done.6
  61.2 3.7 %while.11 = (s32[]{:T(128)}, bf16[4,512,64]{1,2,0:T(8,128)(2,1)S(1)}, bf16[4,512,64]{1,2,0:T(8,128)(2,1)S(1)}, bf16[4,512,64]{1,2,0:T(8,128)(2,1)S(1)}, bf16[4,5...) while((s32[]{:T(128)}, bf16[4,512,64]{1,2,0:T(8,128)(2,1)S(1)}, ...), condition=%wide.region_3.4_spmd.clone, body=%wide.region_0.3_spmd.clone.sunk | while | flops 70024192 | bytes 3424341 | solution.py:98
  62.1 0.4 fusion.115
  63.1 0.4 fusion.115
  64.0 0.4 fusion.115
  64.9 2.9 %convolution_bitcast_fusion = f32[512,1024]{1,0:T(8,128)} fusion(bf16[4,64,1024]{2,1,0:T(8,128)(2,1)} %param.17, bf16[4,512,64]{1,2,0:T(8,128)(2,1)S(1)} %get-tuple-element.34), kind=kOutput, calls=%fused_computation.41 | convolution fusion | flops 268435456 | bytes 2883584 | tf_op jit(solution)/shard_map/nhd,hde->ne/dot_general | solution.py:101
  67.9 10.0 %all-gather.11.cloned.1.call-done = bf16[64,8,1024]{2,1,0:T(8,128)(2,1)} async-done(((bf16[8,8,1024]{2,1,0:T(8,128)(2,1)}), bf16[64,8,1024]{2,1,0:T(8,128)(2,1)}) %all-gather.11.cloned.1.call-update) | async-done | bytes 1048592 | tf_op jit(solution)/shard_map/all_gather | solution.py:42
  78.0 41.6 %all-gather.15.cloned.1.call-done = bf16[64,8,1024]{2,1,0:T(8,128)(2,1)} async-done(((bf16[8,8,1024]{2,1,0:T(8,128)(2,1)}), bf16[64,8,1024]{2,1,0:T(8,128)(2,1)}) %all-gather.15.cloned.1.call-update) | async-done | bytes 1048592 | tf_op jit(solution)/shard_map/all_gather | solution.py:42
  119.7 1.2 fusion.64
  120.9 1.2 multiply_reduce_fusion.1
  122.2 1.9 scatter_custom_fusion
  124.1 16.0 %all_to_all.10 = bf16[8,16,1024]{2,1,0:T(8,128)(2,1)S(1)} all-to-all(bf16[8,16,1024]{2,1,0:T(8,128)(2,1)S(1)} %bitcast.97), channel_id=1, replica_groups=mesh['rz'=8,'ry'=8,'rc'=2,'grp'=4] {'rz'}, dimensions={0} | all-to-all | bytes 524288 | tf_op jit(solution)/shard_map/all_to_all | solution.py:109
  140.3 21.8 %all_to_all.11 = bf16[8,16,1024]{2,0,1:T(8,128)(2,1)S(1)} all-to-all(bf16[8,16,1024]{2,0,1:T(8,128)(2,1)S(1)} %copy.43), channel_id=1, replica_groups=mesh['rz'=8,'ry'=8,'rc'=2,'grp'=4] {'ry','rc'}, dimensions={1} | all-to-all | bytes 524288 | tf_op jit(solution)/shard_map/all_to_all | solution.py:110
  162.2 3.0 %collective-permute-start = (bf16[128,1024]{1,0:T(8,128)(2,1)S(1)}, bf16[128,1024]{1,0:T(8,128)(2,1)S(1)}, u32[]{:S(2)}, u32[]{:S(2)}) collective-permute-start(bf16[128,1024]{1,0:T(8,128)(2,1)S(1)} %bitcast.86), channel_id=1, source_target_pairs={{0,1},{1,2},{2,3},{3,0},{4,5},{5,6},{6,7},{7,4},{8,9},{9,10},{10,1... | collective-permute-start | bytes 786440 | tf_op jit(solution)/shard_map/ppermute | solution.py:120
  165.3 3.4 %collective-permute-start.2 = (bf16[128,1024]{1,0:T(8,128)(2,1)S(1)}, bf16[128,1024]{1,0:T(8,128)(2,1)S(1)}, u32[]{:S(2)}, u32[]{:S(2)}) collective-permute-start(bf16[128,1024]{1,0:T(8,128)(2,1)S(1)} %bitcast.87), channel_id=1, source_target_pairs={{1,0},{2,1},{3,2},{0,3},{5,4},{6,5},{7,6},{4,7},{9,8},{10,9},{11,1... | collective-permute-start | bytes 786440 | tf_op jit(solution)/shard_map/ppermute | solution.py:122
  168.7 4.8 %collective-permute-done = bf16[128,1024]{1,0:T(8,128)(2,1)S(1)} collective-permute-done((bf16[128,1024]{1,0:T(8,128)(2,1)S(1)}, bf16[128,1024]{1,0:T(8,128)(2,1)S(1)}, u32[]{:S(2)}, u32[]{:S(2)}) %collective-permute-start) | collective-permute-done | bytes 262176 | tf_op jit(solution)/shard_map/ppermute | solution.py:120
  173.5 2.1 collective-permute-start.1
  175.7 3.2 %copy.46 = bf16[8,8,2,8,1024]{4,3,2,1,0:T(8,128)(2,1)} copy(bf16[8,8,2,8,1024]{4,3,1,0,2:T(8,128)(2,1)} %bitcast.89) | data formatting | bytes 4194304 | tf_op jit(solution)/shard_map/transpose | solution.py:45
  178.8 3.2 %copy.47 = bf16[8,8,2,8,1024]{4,3,2,1,0:T(8,128)(2,1)} copy(bf16[8,8,2,8,1024]{4,3,0,1,2:T(8,128)(2,1)} %bitcast.90) | data formatting | bytes 4194304 | tf_op jit(solution)/shard_map/transpose | solution.py:47
  182.0 1.9 collective-permute-done.1
  183.9 1.1 pad_maximum_fusion
  185.1 2.8 %gather_fusion = bf16[4,128,1024]{2,1,0:T(8,128)(2,1)} fusion(bf16[4,128,1024]{2,1,0:T(8,128)(2,1)} %pad_maximum_fusion, s32[1024]{0:T(1024)S(1)} %pad_clamp_fusion), kind=kCustom, calls=%fused_computation | custom fusion | bytes 2097168 | tf_op jit(solution)/shard_map/gather | solution.py:125
  187.9 10.1 %fusion.25 = f32[512,1024]{1,0:T(8,128)} fusion(bf16[1024,1024]{1,0:T(8,128)(2,1)} %bitcast.92, bf16[512,1024]{1,0:T(8,128)(2,1)} %bitcast.94, bf16[1024,1024]{1,0:T(8,128)(2,1)} %bitcast.91), kind=kOutput, calls=%fused_computation.42 | convolution fusion | flops 2181562368 | bytes 7340032 | tf_op jit(solution)/shard_map/dot_general | solution.py:132
  198.8 0.8 scatter_fusion
  199.5 1.2 copy.49
  200.8 22.0 %reduce-scatter.5.cloned.1.call-done = f32[128,1024]{1,0:T(8,128)} async-done(((f32[512,1024]{1,0:T(8,128)}), f32[128,1024]{1,0:T(8,128)}) %reduce-scatter.5.cloned.1.call-update) | async-done | bytes 524304 | tf_op jit(solution)/shard_map/reduce_scatter | solution.py:135
  222.7 1.2 fusion.63
  223.9 1.2 multiply_reduce_fusion
  225.2 1.9 add_convert_fusion
  (59 shorter events, 4.1 us)
Async XLA Ops:
  8.0 50.3 %copy-start = (bf16[1024,4,192]{0,2,1:T(8,128)(2,1)S(1)}, bf16[1024,4,192]{0,2,1:T(8,128)(2,1)}, u32[]{:S(2)}) copy-start(bf16[1024,4,192]{0,2,1:T(8,128)(2,1)} %param.16) | copy-start | bytes 4718596
  8.0 69.9 %all-gather.11.cloned.1.call-start = ((), (), s32[]{:S(2)}) async-start(), calls=%async_computation.6 | async-start | bytes 1179648 | tf_op jit(solution)/shard_map/all_gather | solution.py:42
  31.1 88.5 %all-gather.15.cloned.1.call-start = ((), (), s32[]{:S(2)}) async-start(), calls=%async_computation.8 | async-start | bytes 1179648 | tf_op jit(solution)/shard_map/all_gather | solution.py:42
  58.2 61.5 %reduce-scatter.3.cloned.1.call-start = ((), (), s32[]{:S(2)}) async-start(), calls=%async_computation.4 | async-start | bytes 2621440 | tf_op jit(solution)/shard_map/reduce_scatter | solution.py:104
  60.5 0.7 copy-start.6
  67.8 10.2 %copy-start.7 = (s32[1,1,128]{2,1,0:T(1,128)S(1)}, s32[1,1,128]{2,1,0:T(1,128)}, u32[]{:S(2)}) copy-start(s32[1,1,128]{2,1,0:T(1,128)} %param.25) | copy-start | bytes 1540
  67.8 51.9 %copy-start.1 = (bf16[512,1024]{1,0:T(8,128)(2,1)S(1)}, bf16[512,1024]{1,0:T(8,128)(2,1)}, u32[]{:S(2)}) copy-start(bf16[512,1024]{1,0:T(8,128)(2,1)} %param.14) | copy-start | bytes 3145732
  67.8 54.3 %copy-start.2 = (f32[1024]{0:T(1024)S(1)}, f32[1024]{0:T(1024)}, u32[]{:S(2)}) copy-start(f32[1024]{0:T(1024)} %param.19) | copy-start | bytes 12292
  67.9 54.3 %copy-start.3 = (f32[1024]{0:T(1024)S(1)}, f32[1024]{0:T(1024)}, u32[]{:S(2)}) copy-start(f32[1024]{0:T(1024)} %param.18) | copy-start | bytes 12292
  67.9 107.8 %all-gather.13.cloned.1.call-start = ((), (), s32[]{:S(2)}) async-start(), calls=%async_computation.7 | async-start | bytes 3145728 | tf_op jit(solution)/shard_map/all_gather | solution.py:43
  78.0 100.9 %all-gather.17.cloned.1.call-start = ((), (), s32[]{:S(2)}) async-start(), calls=%async_computation.9 | async-start | bytes 3145728 | tf_op jit(solution)/shard_map/all_gather | solution.py:43
  119.6 103.1 %reduce-scatter.5.cloned.1.call-start = ((), (), s32[]{:S(2)}) async-start(), calls=%async_computation.5 | async-start | bytes 2621440 | tf_op jit(solution)/shard_map/reduce_scatter | solution.py:135
  162.2 11.3 %collective-permute-start = (bf16[128,1024]{1,0:T(8,128)(2,1)S(1)}, bf16[128,1024]{1,0:T(8,128)(2,1)S(1)}, u32[]{:S(2)}, u32[]{:S(2)}) collective-permute-start(bf16[128,1024]{1,0:T(8,128)(2,1)S(1)} %bitcast.86), channel_id=1, source_target_pairs={{0,1},{1,2},{2,3},{3,0},{4,5},{5,6},{6,7},{7,4},{8,9},{9,10},{10,1... | collective-permute-start | bytes 786440 | tf_op jit(solution)/shard_map/ppermute | solution.py:120
  165.3 16.8 %collective-permute-start.2 = (bf16[128,1024]{1,0:T(8,128)(2,1)S(1)}, bf16[128,1024]{1,0:T(8,128)(2,1)S(1)}, u32[]{:S(2)}, u32[]{:S(2)}) collective-permute-start(bf16[128,1024]{1,0:T(8,128)(2,1)S(1)} %bitcast.87), channel_id=1, source_target_pairs={{1,0},{2,1},{3,2},{0,3},{5,4},{6,5},{7,6},{4,7},{9,8},{10,9},{11,1... | collective-permute-start | bytes 786440 | tf_op jit(solution)/shard_map/ppermute | solution.py:122
  173.5 10.4 %collective-permute-start.1 = (bf16[128,1024]{1,0:T(8,128)(2,1)S(1)}, bf16[128,1024]{1,0:T(8,128)(2,1)S(1)}, u32[]{:S(2)}, u32[]{:S(2)}) collective-permute-start(bf16[128,1024]{1,0:T(8,128)(2,1)S(1)} %collective-permute-done), channel_id=1, source_target_pairs={{0,1},{1,2},{2,3},{3,0},{4,5},{5,6},{6,7},{7,4},{8,9},{9,10},{10,1... | collective-permute-start | bytes 786440 | tf_op jit(solution)/shard_map/ppermute | solution.py:120
  198.0 0.7 copy-start.8
  198.7 26.4 %copy-start.4 = (f32[1024]{0:T(1024)S(1)}, f32[1024]{0:T(1024)}, u32[]{:S(2)}) copy-start(f32[1024]{0:T(1024)} %param.23) | copy-start | bytes 12292
  198.8 26.4 %copy-start.5 = (f32[1024]{0:T(1024)S(1)}, f32[1024]{0:T(1024)}, u32[]{:S(2)}) copy-start(f32[1024]{0:T(1024)} %param.22) | copy-start | bytes 12292
Sparse Core Ops, SparseCore 0:
  31.2 46.7 all-gather.10
  80.0 39.5 all-gather.14
  121.7 22.7 all-gather.12
  146.4 20.0 all-gather.16
Sparse Core Ops, SparseCore 1:
  67.9 44.0 reduce-scatter.2
  198.1 24.6 reduce-scatter.4
